TPU v7x, 256 devices: a whole 4x4x8 slice. The times are simulated.
256 devices in a mesh: row: 32 (over z, y), col: 8 (over x, core).
Axes of the slice: x: 4, y: 4, z: 8, core: 2. Of those that a mesh axis runs over, the one named last changes fastest.
Arguments:
- saved_input: bfloat16 [1024, 49152], P('col', 'row'), may hold values from -6 to 6
- out_grad: bfloat16 [1024, 12288], P('row', 'col'), may hold values from -0.75 to 0.75
- weight: bfloat16 [49152, 12288], P('row', 'col'), may hold values from -0.625 to 0.625
Outputs:
- in_grad: bfloat16 [1024, 49152], P('col', 'row')
- weight_grad: bfloat16 [49152, 12288], P('row', 'col')
All inputs are finite; a program needn't handle non-finite values.
Results may differ from a plain program's by a relative error of at most 0.0051.
Values may be sent and summed in bfloat16 or wider, within the bound.
No kernel may reach another device: no remote copies, remote signals or barrier semaphores. Data moves between devices by JAX's collectives and lax.ppermute only.
A program may use at most 64 MiB of HBM per device.

v0:
```python
import math
import jax
import jax.numpy as jnp
from jax import lax
from jax.sharding import PartitionSpec as P


def gelu_parts(values):
    coeff = math.sqrt(2.0 / math.pi)
    inner = jnp.tanh(coeff * (values + 0.044715 * values * values * values))
    gelu_value = 0.5 * values * (1.0 + inner)
    gelu_slope = 0.5 * (1.0 + inner) + 0.5 * values * (1.0 - inner * inner) * coeff * (
        1.0 + 3.0 * 0.044715 * values * values
    )
    return (gelu_value, gelu_slope)


def per_device(saved_input, out_grad, weight):
    grad_all = lax.all_gather(out_grad, "row", axis=0, tiled=True)
    saved_all = lax.all_gather(saved_input, "col", axis=0, tiled=True)
    gelu_value, unused_slope = gelu_parts(saved_all.astype(jnp.float32))
    hidden = gelu_value.astype(jnp.bfloat16)
    weight_grad = lax.dot_general(
        hidden, grad_all, (((0,), (0,)), ((), ())), preferred_element_type=jnp.float32
    ).astype(jnp.bfloat16)
    back = lax.psum_scatter(
        lax.dot_general(
            grad_all, weight, (((1,), (1,)), ((), ())), preferred_element_type=jnp.float32
        ),
        "col",
        scatter_dimension=0,
        tiled=True,
    )
    unused_value, own_slope = gelu_parts(saved_input.astype(jnp.float32))
    in_grad = (back * own_slope).astype(jnp.bfloat16)
    return (in_grad, weight_grad)


def solution(mesh):
    in_specs = (P("col", "row"), P("row", "col"), P("row", "col"))
    out_specs = (P("col", "row"), P("row", "col"))
    return jax.shard_map(
        per_device, mesh=mesh, in_specs=in_specs, out_specs=out_specs, check_vma=False
    )
```

profile of v0, /device:TPU:1, one launch (start us, length us, event | category | flops | bytes accessed | tf_op | source)
XLA Modules:
  0.0 178.5 jit_solution(13680003618552402031)
XLA Ops:
  7.2 0.0 all-gather.3.cloned.1.call-start
  7.2 0.7 all-gather.3.cloned.1.call-update
  7.9 0.0 all-gather.5.cloned.1.call-start
  7.9 0.7 all-gather.5.cloned.1.call-update
  8.6 0.0 reduce-scatter.2.cloned.1.call-start
  8.7 81.3 %all-gather.3.cloned.1.call-done = bf16[1024,1536]{1,0:T(8,128)(2,1)} async-done(((bf16[32,1536]{1,0:T(8,128)(2,1)}), bf16[1024,1536]{1,0:T(8,128)(2,1)}) %all-gather.3.cloned.1.call-update) | async-done | bytes 3145744 | tf_op jit(solution)/shard_map/all_gather | solution.py:19
  90.0 9.8 %fusion.23 = f32[1024,1536]{1,0:T(8,128)} fusion(bf16[1024,1536]{1,0:T(8,128)(2,1)} %all-gather.3.cloned.1.call-done, bf16[1536,1536]{1,0:T(8,128)(2,1)} %param.5), kind=kOutput, calls=%fused_computation.35 | convolution fusion | flops 4831838208 | bytes 14155776 | tf_op jit(solution)/shard_map/dot_general | solution.py:27
  99.7 0.0 copy-start.1
  99.7 0.0 reduce-scatter.2.cloned.1.call-update
  99.8 0.0 copy-start
  99.8 23.2 %all-gather.5.cloned.1.call-done = bf16[1024,1536]{1,0:T(8,128)(2,1)} async-done(((bf16[128,1536]{1,0:T(8,128)(2,1)}), bf16[1024,1536]{1,0:T(8,128)(2,1)}) %all-gather.5.cloned.1.call-update) | async-done | bytes 3145744 | tf_op jit(solution)/shard_map/all_gather | solution.py:20
  122.9 0.0 copy-done.1
  122.9 11.2 %convolution_convert_fusion = bf16[1536,1536]{1,0:T(8,128)(2,1)} fusion(bf16[1024,1536]{1,0:T(8,128)(2,1)S(1)} %copy-done.1, bf16[1024,1536]{1,0:T(8,128)(2,1)} %all-gather.5.cloned.1.call-done), kind=kOutput, calls=%fused_computation.5 | convolution fusion | flops 4849926144 | bytes 11010048 | tf_op jit(solution)/shard_map/dot_general | solution.py:23
  134.2 35.4 %reduce-scatter.2.cloned.1.call-done = f32[128,1536]{1,0:T(8,128)} async-done(((f32[1024,1536]{1,0:T(8,128)}), f32[128,1536]{1,0:T(8,128)}) %reduce-scatter.2.cloned.1.call-update) | async-done | bytes 786448 | tf_op jit(solution)/shard_map/reduce_scatter | solution.py:26
  169.6 0.0 copy-done
  169.6 2.4 %fusion.17 = bf16[128,1536]{1,0:T(8,128)(2,1)} fusion(f32[128,1536]{1,0:T(8,128)} %reduce-scatter.2.cloned.1.call-done, bf16[128,1536]{1,0:T(8,128)(2,1)S(1)} %copy-done), kind=kLoop, calls=%fused_computation.29 | loop fusion | flops 3932160 | bytes 1572864 | tf_op jit(solution)/shard_map/convert_element_type | solution.py:35
Async XLA Ops:
  7.2 82.8 %all-gather.3.cloned.1.call-start = ((), (), s32[]{:S(2)}) async-start(), calls=%async_computation.1 | async-start | bytes 3244032 | tf_op jit(solution)/shard_map/all_gather | solution.py:19
  7.9 115.0 %all-gather.5.cloned.1.call-start = ((), (), s32[]{:S(2)}) async-start(), calls=%async_computation.3 | async-start | bytes 3538944 | tf_op jit(solution)/shard_map/all_gather | solution.py:20
  8.6 161.0 %reduce-scatter.2.cloned.1.call-start = ((), (), s32[]{:S(2)}) async-start(), calls=%async_computation.2 | async-start | bytes 7077888 | tf_op jit(solution)/shard_map/reduce_scatter | solution.py:26
  99.7 23.2 %copy-start.1 = (bf16[1024,1536]{1,0:T(8,128)(2,1)S(1)}, bf16[1024,1536]{1,0:T(8,128)(2,1)}, u32[]{:S(2)}) copy-start(bf16[1024,1536]{1,0:T(8,128)(2,1)} %all-gather.3.cloned.1.call-done) | copy-start | bytes 9437188
  99.8 69.8 %copy-start = (bf16[128,1536]{1,0:T(8,128)(2,1)S(1)}, bf16[128,1536]{1,0:T(8,128)(2,1)}, u32[]{:S(2)}) copy-start(bf16[128,1536]{1,0:T(8,128)(2,1)} %param.3) | copy-start | bytes 1179652
Sparse Core Ops, SparseCore 0:
  10.5 79.3 all-gather.2
  91.8 31.1 all-gather.4
  125.5 44.0 reduce-scatter.1
where the time goes:
time: 179 us
  waiting for transfers between devices  141 us (79%)
  matrix products  21 us (12%)
  between operations  13.8 us (8%)
  other arithmetic  2.4 us (1%)
    all_gather x1, waiting for transfers between devices, per_device(): grad_all = lax.all_gather(out_grad, 'row', axis=0, tiled=True)  81.3 us
    reduce_scatter x1, waiting for transfers between devices, per_device(): lax.psum_scatter(lax.dot_general(grad_all, weight, (((1,), (1,)), ((), ()...  35.4 us
    all_gather x1, waiting for transfers between devices, per_device(): saved_all = lax.all_gather(saved_input, 'col', axis=0, tiled=True)  23.2 us
    dot_general x1, matrix products, per_device(): lax.dot_general(hidden, grad_all, (((0,), (0,)), ((), ())), preferred_ele...  11.2 us
    dot_general x1, matrix products, per_device(): lax.dot_general(grad_all, weight, (((1,), (1,)), ((), ())), preferred_ele...  9.78 us
  transfers between devices with their start and end apart: 3, of which 3 were waited for; matrix products, arithmetic and copies ran while one was open for 12% of the time, Pallas kernels for 0%

commit v1 on v0

--- a/solution.py
+++ b/solution.py
@@ -3,6 +3,22 @@
 import jax.numpy as jnp
 from jax import lax
 from jax.sharding import PartitionSpec as P
+
+
+def _carry_side(message):
+    k_all = jax.lax.axis_size("col")
+    line_up = [(idx, (idx + 1) % k_all) for idx in range(k_all)]
+    later, then = ([message], [message])
+    runs = [(idx, (idx - 1) % k_all) for idx in range(k_all)]
+    for _ in range(k_all // 2):
+        later.append(jax.lax.ppermute(later[-1], axis_name="col", perm=line_up))
+    for _ in range((k_all - 1) // 2):
+        then.append(jax.lax.ppermute(then[-1], axis_name="col", perm=runs))
+    return jnp.roll(
+        jnp.concatenate([*later[::-1], *then[1:]], axis=0),
+        (jax.lax.axis_index("col") - k_all // 2) * message.shape[0],
+        axis=0,
+    )
 
 
 def gelu_parts(values):
@@ -17,7 +33,7 @@
 
 def per_device(saved_input, out_grad, weight):
     grad_all = lax.all_gather(out_grad, "row", axis=0, tiled=True)
-    saved_all = lax.all_gather(saved_input, "col", axis=0, tiled=True)
+    saved_all = _carry_side(saved_input)
     gelu_value, unused_slope = gelu_parts(saved_all.astype(jnp.float32))
     hidden = gelu_value.astype(jnp.bfloat16)
     weight_grad = lax.dot_general(

time: 179 us -> 168 us (0.939)
  waiting for transfers between devices: 141 us -> 116 us
  starting transfers between devices: 0.11 us -> 16 us
  matrix products: 21 us -> 17.1 us
    reduce_scatter x1, waiting for transfers between devices: 35.4 us -> 0.68 us  [per_device(): lax.psum_scatter(lax.dot_general(grad_all, weight, (((1,), (1,)), ((), ()...]
    ppermute x0 -> x7, waiting for transfers between devices: none -> 32.3 us  [the longest x4 27.6 us: _carry_side(): later.append(jax.lax.ppermute(later[-1], axis_name='col', perm=line_up))]
    all_gather x1 -> x0, waiting for transfers between devices: 23.2 us -> none  [per_device(): saved_all = lax.all_gather(saved_input, 'col', axis=0, tiled=True)]
    ppermute x0 -> x7, starting transfers between devices: none -> 16 us  [the longest x4 13.1 us: _carry_side(): later.append(jax.lax.ppermute(later[-1], axis_name='col', perm=line_up))]
    dot_general x1, matrix products: 11.2 us -> 7.36 us  [per_device(): lax.dot_general(hidden, grad_all, (((0,), (0,)), ((), ())), preferred_ele...]
  transfers between devices with their start and end apart: 3 -> 9, of which waited for: 3 -> 9; matrix products, arithmetic and copies ran while one was open for 12% -> 5% of each run, Pallas kernels for 0% -> 0%
where the time goes in v1:
time: 168 us; the launch traced here: 167 us
  waiting for transfers between devices  116 us (69%)
  matrix products  17.1 us (10%)
  starting transfers between devices  16 us (10%)
  between operations  14.2 us (8%)
  other arithmetic  2.4 us (1%)
    all_gather x1, waiting for transfers between devices, per_device(): grad_all = lax.all_gather(out_grad, 'row', axis=0, tiled=True)  82 us
    ppermute x4, waiting for transfers between devices, _carry_side(): later.append(jax.lax.ppermute(later[-1], axis_name='col', perm=line_up))  27.6 us
    ppermute x4, starting transfers between devices, _carry_side(): later.append(jax.lax.ppermute(later[-1], axis_name='col', perm=line_up))  13.1 us
    dot_general x1, matrix products, per_device(): lax.dot_general(grad_all, weight, (((1,), (1,)), ((), ())), preferred_ele...  9.76 us
    dot_general x1, matrix products, per_device(): lax.dot_general(hidden, grad_all, (((0,), (0,)), ((), ())), preferred_ele...  7.36 us
    ppermute x3, waiting for transfers between devices, _carry_side(): then.append(jax.lax.ppermute(then[-1], axis_name='col', perm=runs))  4.63 us
  transfers between devices with their start and end apart: 9, of which 9 were waited for; matrix products, arithmetic and copies ran while one was open for 5% of the time, Pallas kernels for 0%

profile of v1, /device:TPU:1, one launch (start us, length us, event | category | flops | bytes accessed | tf_op | source)
XLA Modules:
  0.0 166.8 jit_solution(2828911500196782964)
XLA Ops:
  7.2 0.0 all-gather.2.cloned.1.call-start
  7.2 0.7 all-gather.2.cloned.1.call-update
  7.9 0.0 reduce-scatter.2.cloned.1.call-start
  7.9 82.0 %all-gather.2.cloned.1.call-done = bf16[1024,1536]{1,0:T(8,128)(2,1)} async-done(((bf16[32,1536]{1,0:T(8,128)(2,1)}), bf16[1024,1536]{1,0:T(8,128)(2,1)}) %all-gather.2.cloned.1.call-update) | async-done | bytes 3145744 | tf_op jit(solution)/shard_map/all_gather | solution.py:35
  90.0 9.8 %fusion.25 = f32[1024,1536]{1,0:T(8,128)} fusion(bf16[1024,1536]{1,0:T(8,128)(2,1)} %all-gather.2.cloned.1.call-done, bf16[1536,1536]{1,0:T(8,128)(2,1)} %param.5), kind=kOutput, calls=%fused_computation.53 | convolution fusion | flops 4831838208 | bytes 14155776 | tf_op jit(solution)/shard_map/dot_general | solution.py:43
  99.7 0.0 copy-start
  99.7 0.0 reduce-scatter.2.cloned.1.call-update
  99.7 1.0 copy-done
  100.7 5.6 %collective-permute-start = (bf16[128,1536]{1,0:T(8,128)(2,1)S(1)}, bf16[128,1536]{1,0:T(8,128)(2,1)S(1)}, u32[]{:S(2)}, u32[]{:S(2)}) collective-permute-start(bf16[128,1536]{1,0:T(8,128)(2,1)S(1)} %copy-done), channel_id=1, source_target_pairs={{0,1},{1,2},{2,3},{3,4},{4,5},{5,6},{6,7},{7,0},{8,9},{9,10},{10,1... | collective-permute-start | bytes 1179656 | tf_op jit(solution)/shard_map/ppermute | solution.py:14
  106.4 4.7 %collective-permute-done = bf16[128,1536]{1,0:T(8,128)(2,1)S(1)} collective-permute-done((bf16[128,1536]{1,0:T(8,128)(2,1)S(1)}, bf16[128,1536]{1,0:T(8,128)(2,1)S(1)}, u32[]{:S(2)}, u32[]{:S(2)}) %collective-permute-start) | collective-permute-done | bytes 393248 | tf_op jit(solution)/shard_map/ppermute | solution.py:14
  111.1 2.5 %collective-permute-start.1 = (bf16[128,1536]{1,0:T(8,128)(2,1)S(1)}, bf16[128,1536]{1,0:T(8,128)(2,1)S(1)}, u32[]{:S(2)}, u32[]{:S(2)}) collective-permute-start(bf16[128,1536]{1,0:T(8,128)(2,1)S(1)} %collective-permute-done), channel_id=1, source_target_pairs={{0,1},{1,2},{2,3},{3,4},{4,5},{5,6},{6,7},{7,0},{8,9},{9,10},{10,1... | collective-permute-start | bytes 1179656 | tf_op jit(solution)/shard_map/ppermute | solution.py:14
  113.6 0.1 collective-permute-start.4
  113.7 8.9 %collective-permute-done.1 = bf16[128,1536]{1,0:T(8,128)(2,1)S(1)} collective-permute-done((bf16[128,1536]{1,0:T(8,128)(2,1)S(1)}, bf16[128,1536]{1,0:T(8,128)(2,1)S(1)}, u32[]{:S(2)}, u32[]{:S(2)}) %collective-permute-start.1) | collective-permute-done | bytes 393248 | tf_op jit(solution)/shard_map/ppermute | solution.py:14
  122.6 2.5 %collective-permute-start.2 = (bf16[128,1536]{1,0:T(8,128)(2,1)S(1)}, bf16[128,1536]{1,0:T(8,128)(2,1)S(1)}, u32[]{:S(2)}, u32[]{:S(2)}) collective-permute-start(bf16[128,1536]{1,0:T(8,128)(2,1)S(1)} %collective-permute-done.1), channel_id=1, source_target_pairs={{0,1},{1,2},{2,3},{3,4},{4,5},{5,6},{6,7},{7,0},{8,9},{9,10},{10,1... | collective-permute-start | bytes 1179656 | tf_op jit(solution)/shard_map/ppermute | solution.py:14
  125.0 0.4 collective-permute-done.4
  125.4 1.0 collective-permute-start.5
  126.4 7.6 %collective-permute-done.2 = bf16[128,1536]{1,0:T(8,128)(2,1)S(1)} collective-permute-done((bf16[128,1536]{1,0:T(8,128)(2,1)S(1)}, bf16[128,1536]{1,0:T(8,128)(2,1)S(1)}, u32[]{:S(2)}, u32[]{:S(2)}) %collective-permute-start.2) | collective-permute-done | bytes 393248 | tf_op jit(solution)/shard_map/ppermute | solution.py:14
  134.0 2.5 %collective-permute-start.3 = (bf16[128,1536]{1,0:T(8,128)(2,1)S(1)}, bf16[128,1536]{1,0:T(8,128)(2,1)S(1)}, u32[]{:S(2)}, u32[]{:S(2)}) collective-permute-start(bf16[128,1536]{1,0:T(8,128)(2,1)S(1)} %collective-permute-done.2), channel_id=1, source_target_pairs={{0,1},{1,2},{2,3},{3,4},{4,5},{5,6},{6,7},{7,0},{8,9},{9,10},{10,1... | collective-permute-start | bytes 1179656 | tf_op jit(solution)/shard_map/ppermute | solution.py:14
  136.5 0.0 copy-start.1
  136.5 0.8 collective-permute-done.5
  137.3 1.8 %collective-permute-start.6 = (bf16[128,1536]{1,0:T(8,128)(2,1)S(1)}, bf16[128,1536]{1,0:T(8,128)(2,1)S(1)}, u32[]{:S(2)}, u32[]{:S(2)}) collective-permute-start(bf16[128,1536]{1,0:T(8,128)(2,1)S(1)} %collective-permute-done.5), channel_id=1, source_target_pairs={{0,7},{1,0},{2,1},{3,2},{4,3},{5,4},{6,5},{7,6},{8,15},{9,8},{10,9... | collective-permute-start | bytes 1179656 | tf_op jit(solution)/shard_map/ppermute | solution.py:16
  139.1 6.4 %collective-permute-done.3 = bf16[128,1536]{1,0:T(8,128)(2,1)S(1)} collective-permute-done((bf16[128,1536]{1,0:T(8,128)(2,1)S(1)}, bf16[128,1536]{1,0:T(8,128)(2,1)S(1)}, u32[]{:S(2)}, u32[]{:S(2)}) %collective-permute-start.3) | collective-permute-done | bytes 393248 | tf_op jit(solution)/shard_map/ppermute | solution.py:14
  145.8 3.4 %collective-permute-done.6 = bf16[128,1536]{1,0:T(8,128)(2,1)S(1)} collective-permute-done((bf16[128,1536]{1,0:T(8,128)(2,1)S(1)}, bf16[128,1536]{1,0:T(8,128)(2,1)S(1)}, u32[]{:S(2)}, u32[]{:S(2)}) %collective-permute-start.6) | collective-permute-done | bytes 393248 | tf_op jit(solution)/shard_map/ppermute | solution.py:16
  149.5 0.0 copy-done.1
  149.5 7.4 %convolution_convert_fusion = bf16[1536,1536]{1,0:T(8,128)(2,1)} fusion(bf16[1024,1536]{1,0:T(8,128)(2,1)S(1)} %copy-done.1, bf16[2048,1536]{1,0:T(8,128)(2,1)S(1)} %constant_dynamic-update-slice_fusion, s32[]{:T(128)S(6)} %select_n.14), kind=kOutput, calls=%fused_computation.5 | convolution fusion | flops 4849926144 | bytes 11010052 | tf_op jit(solution)/shard_map/dot_general | solution.py:39
  156.9 0.7 reduce-scatter.2.cloned.1.call-done
  157.6 2.4 %fusion.18 = bf16[128,1536]{1,0:T(8,128)(2,1)} fusion(f32[128,1536]{1,0:T(8,128)} %reduce-scatter.2.cloned.1.call-done, bf16[128,1536]{1,0:T(8,128)(2,1)S(1)} %copy-done), kind=kLoop, calls=%fused_computation.30 | loop fusion | flops 3932160 | bytes 1572864 | tf_op jit(solution)/shard_map/convert_element_type | solution.py:51
  (16 shorter events, 0.4 us)
Async XLA Ops:
  7.2 82.8 %all-gather.2.cloned.1.call-start = ((), (), s32[]{:S(2)}) async-start(), calls=%async_computation.1 | async-start | bytes 3244032 | tf_op jit(solution)/shard_map/all_gather | solution.py:35
  7.9 149.7 %reduce-scatter.2.cloned.1.call-start = ((), (), s32[]{:S(2)}) async-start(), calls=%async_computation.2 | async-start | bytes 7077888 | tf_op jit(solution)/shard_map/reduce_scatter | solution.py:42
  99.7 1.0 copy-start
  100.7 10.4 %collective-permute-start = (bf16[128,1536]{1,0:T(8,128)(2,1)S(1)}, bf16[128,1536]{1,0:T(8,128)(2,1)S(1)}, u32[]{:S(2)}, u32[]{:S(2)}) collective-permute-start(bf16[128,1536]{1,0:T(8,128)(2,1)S(1)} %copy-done), channel_id=1, source_target_pairs={{0,1},{1,2},{2,3},{3,4},{4,5},{5,6},{6,7},{7,0},{8,9},{9,10},{10,1... | collective-permute-start | bytes 1179656 | tf_op jit(solution)/shard_map/ppermute | solution.py:14
  111.1 11.5 %collective-permute-start.1 = (bf16[128,1536]{1,0:T(8,128)(2,1)S(1)}, bf16[128,1536]{1,0:T(8,128)(2,1)S(1)}, u32[]{:S(2)}, u32[]{:S(2)}) collective-permute-start(bf16[128,1536]{1,0:T(8,128)(2,1)S(1)} %collective-permute-done), channel_id=1, source_target_pairs={{0,1},{1,2},{2,3},{3,4},{4,5},{5,6},{6,7},{7,0},{8,9},{9,10},{10,1... | collective-permute-start | bytes 1179656 | tf_op jit(solution)/shard_map/ppermute | solution.py:14
  113.6 11.9 %collective-permute-start.4 = (bf16[128,1536]{1,0:T(8,128)(2,1)S(1)}, bf16[128,1536]{1,0:T(8,128)(2,1)S(1)}, u32[]{:S(2)}, u32[]{:S(2)}) collective-permute-start(bf16[128,1536]{1,0:T(8,128)(2,1)S(1)} %copy-done), channel_id=1, source_target_pairs={{0,7},{1,0},{2,1},{3,2},{4,3},{5,4},{6,5},{7,6},{8,15},{9,8},{10,9... | collective-permute-start | bytes 1179656 | tf_op jit(solution)/shard_map/ppermute | solution.py:16
  122.6 11.5 %collective-permute-start.2 = (bf16[128,1536]{1,0:T(8,128)(2,1)S(1)}, bf16[128,1536]{1,0:T(8,128)(2,1)S(1)}, u32[]{:S(2)}, u32[]{:S(2)}) collective-permute-start(bf16[128,1536]{1,0:T(8,128)(2,1)S(1)} %collective-permute-done.1), channel_id=1, source_target_pairs={{0,1},{1,2},{2,3},{3,4},{4,5},{5,6},{6,7},{7,0},{8,9},{9,10},{10,1... | collective-permute-start | bytes 1179656 | tf_op jit(solution)/shard_map/ppermute | solution.py:14
  125.4 11.9 %collective-permute-start.5 = (bf16[128,1536]{1,0:T(8,128)(2,1)S(1)}, bf16[128,1536]{1,0:T(8,128)(2,1)S(1)}, u32[]{:S(2)}, u32[]{:S(2)}) collective-permute-start(bf16[128,1536]{1,0:T(8,128)(2,1)S(1)} %collective-permute-done.4), channel_id=1, source_target_pairs={{0,7},{1,0},{2,1},{3,2},{4,3},{5,4},{6,5},{7,6},{8,15},{9,8},{10,9... | collective-permute-start | bytes 1179656 | tf_op jit(solution)/shard_map/ppermute | solution.py:16
  134.0 11.5 %collective-permute-start.3 = (bf16[128,1536]{1,0:T(8,128)(2,1)S(1)}, bf16[128,1536]{1,0:T(8,128)(2,1)S(1)}, u32[]{:S(2)}, u32[]{:S(2)}) collective-permute-start(bf16[128,1536]{1,0:T(8,128)(2,1)S(1)} %collective-permute-done.2), channel_id=1, source_target_pairs={{0,1},{1,2},{2,3},{3,4},{4,5},{5,6},{6,7},{7,0},{8,9},{9,10},{10,1... | collective-permute-start | bytes 1179656 | tf_op jit(solution)/shard_map/ppermute | solution.py:14
  136.5 13.0 %copy-start.1 = (bf16[1024,1536]{1,0:T(8,128)(2,1)S(1)}, bf16[1024,1536]{1,0:T(8,128)(2,1)}, u32[]{:S(2)}) copy-start(bf16[1024,1536]{1,0:T(8,128)(2,1)} %all-gather.2.cloned.1.call-done) | copy-start | bytes 9437188
  137.3 11.9 %collective-permute-start.6 = (bf16[128,1536]{1,0:T(8,128)(2,1)S(1)}, bf16[128,1536]{1,0:T(8,128)(2,1)S(1)}, u32[]{:S(2)}, u32[]{:S(2)}) collective-permute-start(bf16[128,1536]{1,0:T(8,128)(2,1)S(1)} %collective-permute-done.5), channel_id=1, source_target_pairs={{0,7},{1,0},{2,1},{3,2},{4,3},{5,4},{6,5},{7,6},{8,15},{9,8},{10,9... | collective-permute-start | bytes 1179656 | tf_op jit(solution)/shard_map/ppermute | solution.py:16
Sparse Core Ops, SparseCore 0:
  10.5 79.3 all-gather.1
  99.9 57.6 reduce-scatter.1
